TPU v7x, 32 devices: a whole 2x2x4 slice. The times are simulated.
32 devices in a mesh: seq: 8 (over z, x), tp: 4 (over y, core).
Axes of the slice: x: 2, y: 2, z: 4, core: 2. Of those that a mesh axis runs over, the one named last changes fastest.
Arguments:
- queries: bfloat16 [1024, 4096], P('seq', 'tp'), may hold values from -600 to 600
- suffix_keys: bfloat16 [1024, 1024], P('seq', 'tp'), may hold values from -6 to 6
- suffix_values: bfloat16 [1024, 1024], P('seq', 'tp'), may hold values from -6 to 6
- prefix_keys: bfloat16 [512, 1024], P('seq', 'tp'), may hold values from -6 to 6
- prefix_values: bfloat16 [512, 1024], P('seq', 'tp'), may hold values from -6 to 6
- suffix_lengths: int32 [24], replicated, may hold values from 1 to 128, 1024 in all
- request_group: int32 [24], replicated, may hold values from 0 to 3
- block_group: int32 [8], replicated, may hold values from 0 to 3, as said below
Outputs:
- attended: bfloat16 [1024, 4096], P('seq', 'tp')
- cache_keys: bfloat16 [1024, 1024], P(('seq', 'tp'))
- cache_values: bfloat16 [1024, 1024], P(('seq', 'tp'))
Inputs may be any that keep to these rules, and one draw needn't show every extreme that they name: `suffix_lengths`: the suffixes fill the 1024 packed tokens end to end in order; the longest has exactly 128 tokens. `block_group`: each prefix is held by exactly 2 blocks, in any order.
All inputs are finite; a program needn't handle non-finite values.
Results may differ from a plain program's by a relative error of at most 0.009.
The roundings to bfloat16 on the way count: a program that leaves them out, or rounds other values in their place, can miss the bound.
Values may be sent and summed in bfloat16 or wider, within the bound.
No kernel may reach another device: no remote copies, remote signals or barrier semaphores. Data moves between devices by JAX's collectives and lax.ppermute only.
A program may use at most 64 MiB of HBM per device.

v0:
```python
import math
import jax
import jax.numpy as jnp
from jax import lax
from jax.sharding import PartitionSpec as P

HD = 128
GROUPS = 4
BIG_NEGATIVE = -1e30


def from_behind(array, axis, by):
    length = lax.axis_size(axis)
    pairs = [(i, i + by) for i in range(length) if 0 <= i + by < length]
    return lax.ppermute(array, axis, pairs)


def rotate(values, position):
    half = values.shape[-1] // 2
    freq = jnp.exp(
        jnp.arange(half, dtype=jnp.float32) * (-2.0 * math.log(500000.0) / values.shape[-1])
    )
    angle = position.astype(jnp.float32)[:, None] * freq[None, :]
    cosine = jnp.cos(angle)[:, None, :]
    sine = jnp.sin(angle)[:, None, :]
    floats = values.astype(jnp.float32)
    lower = floats[..., :half]
    upper = floats[..., half:]
    return jnp.concatenate(
        [lower * cosine - upper * sine, upper * cosine + lower * sine], axis=-1
    ).astype(jnp.bfloat16)


def token_info(index, suffix_lengths, request_group):
    ends = jnp.cumsum(suffix_lengths)
    request = jnp.sum((index[:, None] >= ends[None, :]).astype(jnp.int32), axis=1)
    onehot = request[:, None] == jnp.arange(suffix_lengths.shape[0], dtype=jnp.int32)[None, :]
    first = jnp.sum(jnp.where(onehot, (ends - suffix_lengths)[None, :], 0), axis=1)
    group = jnp.sum(jnp.where(onehot, request_group[None, :], 0), axis=1)
    return (request, index - first, group)


def body(
    queries,
    suffix_keys,
    suffix_values,
    prefix_keys,
    prefix_values,
    suffix_lengths,
    request_group,
    block_group,
):
    rows = queries.shape[0]
    kv_cols = suffix_keys.shape[1]
    kv_heads = kv_cols // HD
    q_heads = queries.shape[1] // HD
    repeat = q_heads // kv_heads
    devices = lax.axis_size("seq")
    me = lax.axis_index("seq")
    block_rows = prefix_keys.shape[0]
    prefix_len = block_rows * devices // GROUPS
    span = max(1, min(2048 // rows, devices // 8))
    scale = HD ** (-0.5)
    index = me * rows + jnp.arange(rows, dtype=jnp.int32)
    request, offset, group = token_info(index, suffix_lengths, request_group)
    position = offset + prefix_len
    q_rot = rotate(queries.reshape(rows, q_heads, HD), position).reshape(rows, kv_heads, repeat, HD)
    k_rot = rotate(suffix_keys.reshape(rows, kv_heads, HD), position).reshape(rows, kv_cols)

    def update(carry, keys, values, visible):
        high, total, accum = carry
        keys_split = keys.reshape(keys.shape[0], kv_heads, HD)
        values_split = values.reshape(values.shape[0], kv_heads, HD)
        scores = (
            jnp.einsum("bgrd,kgd->bgrk", q_rot, keys_split, preferred_element_type=jnp.float32)
            * scale
        )
        mask = visible[:, None, None, :]
        scores = jnp.where(mask, scores, BIG_NEGATIVE)
        new_high = jnp.maximum(high, jnp.max(scores, axis=-1))
        weights = jnp.where(mask, jnp.exp(scores - new_high[..., None]), 0.0)
        factor = jnp.exp(high - new_high)
        total = total * factor + jnp.sum(weights, axis=-1)
        accum = accum * factor[..., None] + jnp.einsum(
            "bgrk,kgd->bgrd",
            weights.astype(jnp.bfloat16),
            values_split,
            preferred_element_type=jnp.float32,
        )
        return (new_high, total, accum)

    def guarded(carry, keys, values, visible):
        return update(carry, keys, values, visible)

    def suffix_visible(back):
        key_index = (me - back) * rows + jnp.arange(rows, dtype=jnp.int32)
        key_request, _, _ = token_info(key_index, suffix_lengths, request_group)
        return (
            (key_index[None, :] >= 0)
            & (key_request[None, :] == request[:, None])
            & (key_index[None, :] <= index[:, None])
        )

    start_state = (
        jnp.full((rows, kv_heads, repeat), BIG_NEGATIVE, jnp.float32),
        jnp.zeros((rows, kv_heads, repeat), jnp.float32),
        jnp.zeros((rows, kv_heads, repeat, HD), jnp.float32),
    )
    carry = start_state
    keys = lax.all_gather(prefix_keys, "seq", axis=0, tiled=True)
    values = lax.all_gather(prefix_values, "seq", axis=0, tiled=True)
    count = keys.shape[0]
    width = 512

    def one_step(state, step):
        first = step * width
        keys_part = lax.dynamic_slice_in_dim(keys, first, width, 0)
        values_part = lax.dynamic_slice_in_dim(values, first, width, 0)
        row_index = first + jnp.arange(width, dtype=jnp.int32)
        holder = row_index // block_rows
        matches = holder[:, None] == jnp.arange(block_group.shape[0], dtype=jnp.int32)[None, :]
        row_group = jnp.sum(jnp.where(matches, block_group[None, :], 0), axis=1)
        visible = row_group[None, :] == group[:, None]
        return (guarded(state, keys_part, values_part, visible), None)

    carry, _ = lax.scan(one_step, carry, jnp.arange(count // width, dtype=jnp.int32))
    carry = guarded(carry, k_rot, suffix_values, suffix_visible(0))
    for back in range(1, span + 1):
        earlier_keys, earlier_values = from_behind((k_rot, suffix_values), "seq", back)
        carry = guarded(carry, earlier_keys, earlier_values, suffix_visible(back))
    high, total, accum = carry
    attended = (accum / total[..., None]).reshape(rows, q_heads * HD).astype(jnp.bfloat16)
    cache_keys, cache_values = (
        lax.all_to_all(k_rot, "tp", split_axis=0, concat_axis=1, tiled=True),
        lax.all_to_all(suffix_values, "tp", split_axis=0, concat_axis=1, tiled=True),
    )
    return (attended, cache_keys, cache_values)


def solution(mesh):
    return jax.shard_map(
        body,
        mesh=mesh,
        in_specs=(
            P("seq", "tp"),
            P("seq", "tp"),
            P("seq", "tp"),
            P("seq", "tp"),
            P("seq", "tp"),
            P(),
            P(),
            P(),
        ),
        out_specs=(P("seq", "tp"), P(("seq", "tp"), None), P(("seq", "tp"), None)),
        check_vma=False,
    )
```

profile of v0, /device:TPU:0, one launch (start us, length us, event | category | flops | bytes accessed | tf_op | source)
XLA Modules:
  0.0 101.6 jit_solution(3033059807300362979)
XLA Ops:
  0.7 0.8 copy.95
  1.5 0.1 reduce
  1.6 0.7 sub.87
  2.3 0.1 convert_reduce_fusion
  2.4 0.7 select_reduce_fusion.2
  3.1 0.9 copy.101
  4.1 0.1 copy.129
  4.2 0.1 copy.130
  4.3 0.3 multiply_cosine_fusion
  4.7 0.1 maximum_convert_fusion
  4.7 0.7 copy.106
  5.5 5.5 %collective-permute-start = (bf16[128,256]{0,1:T(8,128)(2,1)}, bf16[128,256]{0,1:T(8,128)(2,1)}, u32[]{:S(2)}, u32[]{:S(2)}) collective-permute-start(bf16[128,256]{0,1:T(8,128)(2,1)} %bitcast.19), channel_id=1, source_target_pairs={{0,4},{4,8},{8,12},{12,16},{16,20},{20,24},{24,28},{1,5},{5,9},{9,... | collective-permute-start | bytes 196616 | tf_op jit(solution)/shard_map/ppermute | solution.py:15
  10.9 3.5 %collective-permute-start.1 = (bf16[128,256]{1,0:T(8,128)(2,1)}, bf16[128,256]{1,0:T(8,128)(2,1)}, u32[]{:S(2)}, u32[]{:S(2)}) collective-permute-start(bf16[128,256]{1,0:T(8,128)(2,1)} %param.10), channel_id=1, source_target_pairs={{0,4},{4,8},{8,12},{12,16},{16,20},{20,24},{24,28},{1,5},{5,9},{9,... | collective-permute-start | bytes 196616 | tf_op jit(solution)/shard_map/ppermute | solution.py:15
  14.4 0.1 copy.110
  14.5 0.0 copy-start.7
  14.5 0.7 convert_element_type.70
  15.2 3.3 %all-to-all-start = ((bf16[4,32,256]{2,1,0:T(8,128)(2,1)}), bf16[4,32,256]{2,1,0:T(8,128)(2,1)S(1)}, u32[]{:S(2)}, u32[]{:S(2)}) async-start(bf16[4,32,256]{2,1,0:T(8,128)(2,1)} %convert_element_type.70), calls=%async_computation | async-start | bytes 131072 | tf_op jit(solution)/shard_map/all_to_all | solution.py:134
  18.5 0.1 copy.133
  18.6 0.0 copy-start.8
  18.7 0.2 fusion.46
  18.9 31.0 %all_gather.6 = bf16[512,256]{1,0:T(8,128)(2,1)S(1)} all-gather(bf16[64,256]{1,0:T(8,128)(2,1)S(1)} %copy-done.7), channel_id=1, replica_groups=mesh['seq'=8,'tp'=4] {'seq'}, dimensions={0}, use_global_device_ids=true | all-gather | bytes 294912 | tf_op jit(solution)/shard_map/all_gather | solution.py:110
  49.8 0.1 copy.98
  50.0 0.2 subtract_convert_fusion
  50.2 0.1 select_reduce_fusion
  50.3 0.1 broadcast_compare_fusion
  50.4 0.8 compare_and_fusion
  51.2 1.2 %bitcast_reduce_fusion = (f32[128,2,4]{0,2,1:T(4,128)}, f32[2,128,4,512]{3,1,2,0:T(8,128)S(1)}) fusion(pred[128,512]{1,0:T(8,128)(4,1)S(1)} %broadcast_compare_fusion, bf16[512,2,128,1]{0,2,3,1:T(8,128)(2,1)S(1)} %bitcast.101, bf16[128,2,4,64]{3,0,2,1:T(8,128)(2,1)S(1)} %bitcast.98, bf16[128,2,4,64]{3,0,2,1:T(8,128)(2,1)S(1)} %bitcast.95), kind=kOutput, calls=%fused_computation.1 | convolution fusion | flops 136313856 | bytes 2691072 | tf_op jit(solution)/shard_map/while/body/eval_jaxpr/bgrd,kgd->bgrk/dot_general | solution.py:75
  52.4 0.9 fusion.49
  53.3 0.6 copy-done.4
  53.9 3.9 %all-to-all-start.1 = ((bf16[4,32,256]{2,1,0:T(8,128)(2,1)}), bf16[4,32,256]{2,1,0:T(8,128)(2,1)}, u32[]{:S(2)}, u32[]{:S(2)}) async-start(bf16[4,32,256]{2,1,0:T(8,128)(2,1)} %bitcast.29), calls=%async_computation.1 | async-start | bytes 131072 | tf_op jit(solution)/shard_map/all_to_all | solution.py:135
  57.8 31.0 %all_gather.7 = bf16[512,256]{1,0:T(8,128)(2,1)S(1)} all-gather(bf16[64,256]{1,0:T(8,128)(2,1)} %param.12), channel_id=1, replica_groups=mesh['seq'=8,'tp'=4] {'seq'}, dimensions={0}, use_global_device_ids=true | all-gather | bytes 294912 | tf_op jit(solution)/shard_map/all_gather | solution.py:111
  88.9 0.9 copy.124
  89.8 0.8 copy.100
  90.7 1.5 %copy.131 = bf16[4,4,8,256]{3,2,0,1:T(8,128)(2,1)} copy(bf16[4,4,8,256]{3,2,1,0:T(8,128)(2,1)} %bitcast.106) | data formatting | bytes 131072 | tf_op jit(solution)/shard_map/all_to_all | solution.py:134
  92.2 1.5 %copy.132 = bf16[4,4,8,256]{3,2,0,1:T(8,128)(2,1)} copy(bf16[4,4,8,256]{3,2,1,0:T(8,128)(2,1)} %bitcast.46) | data formatting | bytes 131072 | tf_op jit(solution)/shard_map/all_to_all | solution.py:135
  93.6 0.0 collective-permute-done
  93.6 1.2 %fusion.48 = (f32[128,2,4]{0,2,1:T(4,128)S(1)}, f32[128,2,4,128]{0,3,2,1:T(8,128)S(1)}) fusion(bf16[128,2,128,1]{0,2,3,1:T(8,128)(2,1)} %bitcast.39, bf16[128,2,4,64]{3,0,2,1:T(8,128)(2,1)S(1)} %bitcast.100, bf16[128,2,4,64]{3,0,2,1:T(8,128)(2,1)S(1)} %bitcast.97, pred[128,128]{0,1:T(8,128)(4,1)} %get-tuple-element.67), kind=kOutput, calls=%fused_computation.88 | convolution fusion | flops 34470912 | bytes 872448 | tf_op jit(solution)/shard_map/bgrd,kgd->bgrk/dot_general | solution.py:75
  94.9 0.7 fusion.44
  95.6 0.1 fusion.21
  95.7 0.0 copy-start.3
  95.7 0.2 convolution_bitcast_fusion.1
  96.0 0.7 fusion.2
  96.7 0.1 fusion.23
  96.9 1.6 %fusion.7 = f32[128,2,4,128]{0,3,2,1:T(8,128)} fusion(f32[128,2,4,128]{0,3,2,1:T(8,128)S(1)} %convolution_bitcast_fusion.1, bf16[512,2,128,1]{0,2,3,1:T(8,128)(2,1)S(1)} %bitcast.104, f32[2,128,4,512]{3,1,2,0:T(8,128)S(1)} %get-tuple-element.76, f32[128,2,4]{0,2,1:T(4,128)S(1)} %get-tuple-element.66, pred[128,512]{1,0:T(8,128)(4,1)S(1)} %broadcast_compare_fusion, ...), kind=kOutput, calls=%fused_computation.13 | convolution fusion | flops 137363456 | bytes 3489792 | tf_op jit(solution)/shard_map/while/body/eval_jaxpr/bgrk,kgd->bgrd/dot_general | solution.py:84
  98.5 0.0 collective-permute-done.1
  98.5 0.9 copy.108
  99.4 1.3 %fusion.14 = bf16[128,2,4,128]{0,3,2,1:T(8,128)(2,1)S(1)} fusion(f32[128,2,4,128]{0,3,2,1:T(8,128)} %fusion.7, bf16[128,2,128,1]{0,2,3,1:T(8,128)(2,1)S(1)} %bitcast.109, f32[128,2,4,128]{0,3,2,1:T(8,128)S(1)} %copy-done.1, f32[128,2,4]{0,2,1:T(4,128)S(1)} %get-tuple-element.52, f32[128,2,4]{0,2,1:T(4,128)S(1)} %get-tuple-element.55, ...), kind=kOutput, calls=%fused_computation.22 | convolution fusion | flops 34340864 | bytes 1400832 | tf_op jit(solution)/shard_map/bgrk,kgd->bgrd/dot_general | solution.py:84
  100.7 0.9 copy.113
  (26 shorter events, 0.2 us)
Async XLA Ops:
  0.6 17.9 %copy-start.2 = (bf16[128,1024]{1,0:T(8,128)(2,1)S(1)}, bf16[128,1024]{1,0:T(8,128)(2,1)}, u32[]{:S(2)}) copy-start(bf16[128,1024]{1,0:T(8,128)(2,1)} %param.8) | copy-start | bytes 786436
  5.5 88.2 %collective-permute-start = (bf16[128,256]{0,1:T(8,128)(2,1)}, bf16[128,256]{0,1:T(8,128)(2,1)}, u32[]{:S(2)}, u32[]{:S(2)}) collective-permute-start(bf16[128,256]{0,1:T(8,128)(2,1)} %bitcast.19), channel_id=1, source_target_pairs={{0,4},{4,8},{8,12},{12,16},{16,20},{20,24},{24,28},{1,5},{5,9},{9,... | collective-permute-start | bytes 196616 | tf_op jit(solution)/shard_map/ppermute | solution.py:15
  10.9 87.5 %collective-permute-start.1 = (bf16[128,256]{1,0:T(8,128)(2,1)}, bf16[128,256]{1,0:T(8,128)(2,1)}, u32[]{:S(2)}, u32[]{:S(2)}) collective-permute-start(bf16[128,256]{1,0:T(8,128)(2,1)} %param.10), channel_id=1, source_target_pairs={{0,4},{4,8},{8,12},{12,16},{16,20},{20,24},{24,28},{1,5},{5,9},{9,... | collective-permute-start | bytes 196616 | tf_op jit(solution)/shard_map/ppermute | solution.py:15
  14.5 4.4 %copy-start.7 = (bf16[64,256]{1,0:T(8,128)(2,1)S(1)}, bf16[64,256]{1,0:T(8,128)(2,1)}, u32[]{:S(2)}) copy-start(bf16[64,256]{1,0:T(8,128)(2,1)} %param.11) | copy-start | bytes 98308
  15.2 38.1 %all-to-all-start = ((bf16[4,32,256]{2,1,0:T(8,128)(2,1)}), bf16[4,32,256]{2,1,0:T(8,128)(2,1)S(1)}, u32[]{:S(2)}, u32[]{:S(2)}) async-start(bf16[4,32,256]{2,1,0:T(8,128)(2,1)} %convert_element_type.70), calls=%async_computation | async-start | bytes 131072 | tf_op jit(solution)/shard_map/all_to_all | solution.py:134
  18.6 31.6 %copy-start.8 = (s32[8]{0:T(128)S(1)}, s32[8]{0:T(128)}, u32[]{:S(2)}) copy-start(s32[8]{0:T(128)} %param.15) | copy-start | bytes 100
  53.3 0.6 copy-start.4
  53.9 38.2 %all-to-all-start.1 = ((bf16[4,32,256]{2,1,0:T(8,128)(2,1)}), bf16[4,32,256]{2,1,0:T(8,128)(2,1)}, u32[]{:S(2)}, u32[]{:S(2)}) async-start(bf16[4,32,256]{2,1,0:T(8,128)(2,1)} %bitcast.29), calls=%async_computation.1 | async-start | bytes 131072 | tf_op jit(solution)/shard_map/all_to_all | solution.py:135
  94.9 2.0 %copy-start = (f32[128,2,4,128]{0,3,2,1:T(8,128)}, f32[128,2,4,128]{0,3,2,1:T(8,128)S(1)}, u32[]{:S(2)}) copy-start(f32[128,2,4,128]{0,3,2,1:T(8,128)S(1)} %get-tuple-element.72) | copy-start | bytes 1572868
  94.9 1.8 %copy-start.5 = (pred[128,128]{0,1:T(8,128)(4,1)S(1)}, pred[128,128]{0,1:T(8,128)(4,1)}, u32[]{:S(2)}) copy-start(pred[128,128]{0,1:T(8,128)(4,1)} %get-tuple-element.67) | copy-start | bytes 49156
  95.7 1.1 %copy-start.6 = (f32[128,2,4]{0,2,1:T(4,128)S(1)}, f32[128,2,4]{0,2,1:T(4,128)}, u32[]{:S(2)}) copy-start(f32[128,2,4]{0,2,1:T(4,128)} %get-tuple-element.75) | copy-start | bytes 12292
  95.7 1.1 %copy-start.3 = (bf16[512,256]{0,1:T(8,128)(2,1)S(1)}, bf16[512,256]{0,1:T(8,128)(2,1)}, u32[]{:S(2)}) copy-start(bf16[512,256]{0,1:T(8,128)(2,1)} %copy.100) | copy-start | bytes 786436
  96.9 2.6 %copy-start.1 = (f32[128,2,4,128]{0,3,2,1:T(8,128)S(1)}, f32[128,2,4,128]{0,3,2,1:T(8,128)}, u32[]{:S(2)}) copy-start(f32[128,2,4,128]{0,3,2,1:T(8,128)} %copy-done) | copy-start | bytes 1572868
where the time goes:
time: 102 us
  blocking collectives  62 us (61%)
  starting transfers between devices  16.1 us (16%)
  local copies, waits for them, and re-layouts  11.1 us (11%)
  matrix products  6.46 us (6%)
  other arithmetic  5.01 us (5%)
    all_gather x1, blocking collectives, body(): values = lax.all_gather(prefix_values, 'seq', axis=0, tiled=True)  31 us
    all_gather x1, blocking collectives, body(): keys = lax.all_gather(prefix_keys, 'seq', axis=0, tiled=True)  31 us
    ppermute x2, starting transfers between devices, from_behind(): return lax.ppermute(array, axis, pairs)  8.92 us
    all_to_all x1, starting transfers between devices, body(): lax.all_to_all(suffix_values, 'tp', split_axis=0, concat_axis=1, tiled=True)  3.89 us
    dot_general x3, matrix products, update(): jnp.einsum('bgrd,kgd->bgrk', q_rot, keys_split, preferred_element_type=jn...  3.34 us
    all_to_all x1, starting transfers between devices, body(): lax.all_to_all(k_rot, 'tp', split_axis=0, concat_axis=1, tiled=True)  3.28 us
    dot_general x3, matrix products, update(): jnp.einsum('bgrk,kgd->bgrd', weights.astype(jnp.bfloat16), values_split,...  3.12 us
    unnamed x23, local copies, waits for them, and re-layouts  2.76 us
  transfers between devices with their start and end apart: 4, of which 0 were waited for; matrix products, arithmetic and copies ran while one was open for 14% of the time, Pallas kernels for 0%

commit v1 on v0

--- a/solution.py
+++ b/solution.py
@@ -107,7 +107,20 @@
         jnp.zeros((rows, kv_heads, repeat, HD), jnp.float32),
     )
     carry = start_state
-    keys = lax.all_gather(prefix_keys, "seq", axis=0, tiled=True)
+
+    def compute_leaf(matrix):
+        num = lax.axis_size("seq")
+        panels = [(kk, (kk + 1) % num) for kk in range(num)]
+
+        def obtain_signs(reply):
+            if len(reply) == num:
+                return reply
+            return obtain_signs([lax.ppermute(reply[0], "seq", panels), *reply])
+
+        state_next = jnp.concatenate(obtain_signs([matrix]), 0)
+        return jnp.roll(state_next, (lax.axis_index("seq") + 1) * matrix.shape[0], 0)
+
+    keys = compute_leaf(prefix_keys)
     values = lax.all_gather(prefix_values, "seq", axis=0, tiled=True)
     count = keys.shape[0]
     width = 512

time: 102 us -> 96.5 us (0.946)
  blocking collectives: 62 us -> 30.7 us
  waiting for transfers between devices: 0.01 us -> 30.4 us
  matrix products: 6.46 us -> 2.42 us
  starting transfers between devices: 16.1 us -> 20 us
  local copies, waits for them, and re-layouts: 11.1 us -> 7.97 us
  other arithmetic: 5.01 us -> 3.54 us
    all_gather x1 -> x0, blocking collectives: 31 us -> none  [body(): keys = lax.all_gather(prefix_keys, 'seq', axis=0, tiled=True)]
    ppermute x0 -> x7, waiting for transfers between devices: none -> 30.4 us  [obtain_signs(): return obtain_signs([lax.ppermute(reply[0], 'seq', panels), *reply])]
    ppermute x0 -> x7, starting transfers between devices: none -> 6.62 us  [obtain_signs(): return obtain_signs([lax.ppermute(reply[0], 'seq', panels), *reply])]
    dot_general x3, matrix products: 3.34 us -> 1.26 us  [update(): jnp.einsum('bgrd,kgd->bgrk', q_rot, keys_split, preferred_element_type=jn...]
    ppermute x2, starting transfers between devices: 8.92 us -> 6.86 us  [from_behind(): return lax.ppermute(array, axis, pairs)]
    dot_general x3, matrix products: 3.12 us -> 1.16 us  [update(): jnp.einsum('bgrk,kgd->bgrd', weights.astype(jnp.bfloat16), values_split,...]
    unnamed x23 -> x12, local copies, waits for them, and re-layouts: 2.76 us -> 3.02 us
  transfers between devices with their start and end apart: 4 -> 11, of which waited for: 0 -> 5; matrix products, arithmetic and copies ran while one was open for 14% -> 9% of each run, Pallas kernels for 0% -> 0%
where the time goes in v1:
time: 96.5 us; the launch traced here: 96.1 us
  blocking collectives  30.7 us (32%)
  waiting for transfers between devices  30.4 us (32%)
  starting transfers between devices  20 us (21%)
  local copies, waits for them, and re-layouts  7.97 us (8%)
  other arithmetic  3.54 us (4%)
  matrix products  2.42 us (3%)
    all_gather x1, blocking collectives, body(): values = lax.all_gather(prefix_values, 'seq', axis=0, tiled=True)  30.7 us
    ppermute x7, waiting for transfers between devices, obtain_signs(): return obtain_signs([lax.ppermute(reply[0], 'seq', panels), *reply])  30.4 us
    ppermute x2, starting transfers between devices, from_behind(): return lax.ppermute(array, axis, pairs)  6.86 us
    ppermute x7, starting transfers between devices, obtain_signs(): return obtain_signs([lax.ppermute(reply[0], 'seq', panels), *reply])  6.62 us
    all_to_all x1, starting transfers between devices, body(): lax.all_to_all(suffix_values, 'tp', split_axis=0, concat_axis=1, tiled=True)  3.29 us
    all_to_all x1, starting transfers between devices, body(): lax.all_to_all(k_rot, 'tp', split_axis=0, concat_axis=1, tiled=True)  3.28 us
    unnamed x12, local copies, waits for them, and re-layouts  3.02 us
  transfers between devices with their start and end apart: 11, of which 5 were waited for; matrix products, arithmetic and copies ran while one was open for 9% of the time, Pallas kernels for 0%

profile of v1, /device:TPU:0, one launch (start us, length us, event | category | flops | bytes accessed | tf_op | source)
XLA Modules:
  0.0 96.1 jit_solution(17891337581044361013)
XLA Ops:
  0.6 0.9 copy.109
  1.6 3.0 %collective-permute-start = (bf16[64,256]{0,1:T(8,128)(2,1)S(1)}, bf16[64,256]{0,1:T(8,128)(2,1)S(1)}, u32[]{:S(2)}, u32[]{:S(2)}) collective-permute-start(bf16[64,256]{0,1:T(8,128)(2,1)S(1)} %copy.109), channel_id=1, source_target_pairs={{0,4},{4,8},{8,12},{12,16},{16,20},{20,24},{24,28},{28,0},{1,5},{5... | collective-permute-start | bytes 98312 | tf_op jit(solution)/shard_map/ppermute | solution.py:118
  4.6 0.7 copy.108
  5.3 0.1 reduce
  5.5 0.7 sub.92
  6.1 0.1 convert_reduce_fusion
  6.2 0.7 select_reduce_fusion.2
  7.0 0.9 copy.117
  7.9 0.1 copy.146
  8.0 0.1 copy.147
  8.1 0.3 multiply_cosine_fusion
  8.5 0.1 maximum_convert_fusion
  8.6 0.1 copy.122
  8.7 3.5 %collective-permute-start.7 = (bf16[128,256]{0,1:T(8,128)(2,1)S(1)}, bf16[128,256]{0,1:T(8,128)(2,1)S(1)}, u32[]{:S(2)}, u32[]{:S(2)}) collective-permute-start(bf16[128,256]{0,1:T(8,128)(2,1)S(1)} %bitcast.108), channel_id=1, source_target_pairs={{0,4},{4,8},{8,12},{12,16},{16,20},{20,24},{24,28},{1,5},{5,9},{9,... | collective-permute-start | bytes 196616 | tf_op jit(solution)/shard_map/ppermute | solution.py:15
  12.2 3.4 %collective-permute-start.8 = (bf16[128,256]{1,0:T(8,128)(2,1)}, bf16[128,256]{1,0:T(8,128)(2,1)S(1)}, u32[]{:S(2)}, u32[]{:S(2)}) collective-permute-start(bf16[128,256]{1,0:T(8,128)(2,1)} %param.10), channel_id=1, source_target_pairs={{0,4},{4,8},{8,12},{12,16},{16,20},{20,24},{24,28},{1,5},{5,9},{9,... | collective-permute-start | bytes 196616 | tf_op jit(solution)/shard_map/ppermute | solution.py:15
  15.7 0.7 convert_element_type.70
  16.4 3.3 %all-to-all-start = ((bf16[4,32,256]{2,1,0:T(8,128)(2,1)}), bf16[4,32,256]{2,1,0:T(8,128)(2,1)S(1)}, u32[]{:S(2)}, u32[]{:S(2)}) async-start(bf16[4,32,256]{2,1,0:T(8,128)(2,1)} %convert_element_type.70), calls=%async_computation | async-start | bytes 131072 | tf_op jit(solution)/shard_map/all_to_all | solution.py:147
  19.7 0.1 copy.150
  19.9 0.2 fusion.44
  20.1 0.2 subtract_convert_fusion
  20.3 0.2 compare_and_fusion
  20.5 1.6 %collective-permute-start.1 = (bf16[64,256]{0,1:T(8,128)(2,1)S(1)}, bf16[64,256]{0,1:T(8,128)(2,1)S(1)}, u32[]{:S(2)}, u32[]{:S(2)}) collective-permute-start(bf16[64,256]{0,1:T(8,128)(2,1)S(1)} %collective-permute-done), channel_id=1, source_target_pairs={{0,4},{4,8},{8,12},{12,16},{16,20},{20,24},{24,28},{28,0},{1,5},{5... | collective-permute-start | bytes 98312 | tf_op jit(solution)/shard_map/ppermute | solution.py:118
  22.1 0.3 fusion.47
  22.4 5.3 %collective-permute-done.1 = bf16[64,256]{0,1:T(8,128)(2,1)S(1)} collective-permute-done((bf16[64,256]{0,1:T(8,128)(2,1)S(1)}, bf16[64,256]{0,1:T(8,128)(2,1)S(1)}, u32[]{:S(2)}, u32[]{:S(2)}) %collective-permute-start.1) | collective-permute-done | bytes 32800 | tf_op jit(solution)/shard_map/ppermute | solution.py:118
  27.7 7.0 %collective-permute-done.2 = bf16[64,256]{0,1:T(8,128)(2,1)S(1)} collective-permute-done((bf16[64,256]{0,1:T(8,128)(2,1)S(1)}, bf16[64,256]{0,1:T(8,128)(2,1)S(1)}, u32[]{:S(2)}, u32[]{:S(2)}) %collective-permute-start.2) | collective-permute-done | bytes 32800 | tf_op jit(solution)/shard_map/ppermute | solution.py:118
  34.7 6.9 %collective-permute-done.3 = bf16[64,256]{0,1:T(8,128)(2,1)S(1)} collective-permute-done((bf16[64,256]{0,1:T(8,128)(2,1)S(1)}, bf16[64,256]{0,1:T(8,128)(2,1)S(1)}, u32[]{:S(2)}, u32[]{:S(2)}) %collective-permute-start.3) | collective-permute-done | bytes 32800 | tf_op jit(solution)/shard_map/ppermute | solution.py:118
  41.6 0.1 broadcast_compare_fusion
  41.7 6.8 %collective-permute-done.4 = bf16[64,256]{0,1:T(8,128)(2,1)S(1)} collective-permute-done((bf16[64,256]{0,1:T(8,128)(2,1)S(1)}, bf16[64,256]{0,1:T(8,128)(2,1)S(1)}, u32[]{:S(2)}, u32[]{:S(2)}) %collective-permute-start.4) | collective-permute-done | bytes 32800 | tf_op jit(solution)/shard_map/ppermute | solution.py:118
  48.6 3.3 %all-to-all-start.1 = ((bf16[4,32,256]{2,1,0:T(8,128)(2,1)}), bf16[4,32,256]{2,1,0:T(8,128)(2,1)S(1)}, u32[]{:S(2)}, u32[]{:S(2)}) async-start(bf16[4,32,256]{2,1,0:T(8,128)(2,1)} %bitcast.29), calls=%async_computation.1 | async-start | bytes 131072 | tf_op jit(solution)/shard_map/all_to_all | solution.py:148
  51.9 30.7 %all_gather.3 = bf16[512,256]{1,0:T(8,128)(2,1)S(1)} all-gather(bf16[64,256]{1,0:T(8,128)(2,1)S(1)} %copy-done.1), channel_id=1, replica_groups=mesh['seq'=8,'tp'=4] {'seq'}, dimensions={0}, use_global_device_ids=true | all-gather | bytes 294912 | tf_op jit(solution)/shard_map/all_gather | solution.py:124
  82.6 0.9 copy.141
  83.6 0.1 copy.115
  83.7 0.6 copy.148
  84.4 0.6 copy.149
  85.0 2.0 %collective-permute-start.6 = (bf16[64,256]{0,1:T(8,128)(2,1)S(1)}, bf16[64,256]{0,1:T(8,128)(2,1)S(1)}, u32[]{:S(2)}, u32[]{:S(2)}) collective-permute-start(bf16[64,256]{0,1:T(8,128)(2,1)S(1)} %collective-permute-done.5), channel_id=1, source_target_pairs={{0,4},{4,8},{8,12},{12,16},{16,20},{20,24},{24,28},{28,0},{1,5},{5... | collective-permute-start | bytes 98312 | tf_op jit(solution)/shard_map/ppermute | solution.py:118
  87.0 0.4 fusion.46
  87.4 0.1 copy.124
  87.5 4.5 %collective-permute-done.6 = bf16[64,256]{0,1:T(8,128)(2,1)S(1)} collective-permute-done((bf16[64,256]{0,1:T(8,128)(2,1)S(1)}, bf16[64,256]{0,1:T(8,128)(2,1)S(1)}, u32[]{:S(2)}, u32[]{:S(2)}) %collective-permute-start.6) | collective-permute-done | bytes 32800 | tf_op jit(solution)/shard_map/ppermute | solution.py:118
  92.0 0.5 concatenate.18
  92.5 0.2 constant_dynamic-slice_fusion
  92.7 0.6 fusion
  93.3 0.1 fusion.19
  93.4 0.2 convolution_bitcast_fusion.1
  93.6 0.5 fusion.1
  94.1 0.1 fusion.21
  94.3 0.7 fusion.6
  95.0 0.3 fusion.13
  95.2 0.9 copy.129
  (29 shorter events, 0.4 us)
Async XLA Ops:
  0.6 19.0 %copy-start = (bf16[128,1024]{1,0:T(8,128)(2,1)S(1)}, bf16[128,1024]{1,0:T(8,128)(2,1)}, u32[]{:S(2)}) copy-start(bf16[128,1024]{1,0:T(8,128)(2,1)} %param.8) | copy-start | bytes 786436
  1.6 18.9 %collective-permute-start = (bf16[64,256]{0,1:T(8,128)(2,1)S(1)}, bf16[64,256]{0,1:T(8,128)(2,1)S(1)}, u32[]{:S(2)}, u32[]{:S(2)}) collective-permute-start(bf16[64,256]{0,1:T(8,128)(2,1)S(1)} %copy.109), channel_id=1, source_target_pairs={{0,4},{4,8},{8,12},{12,16},{16,20},{20,24},{24,28},{28,0},{1,5},{5... | collective-permute-start | bytes 98312 | tf_op jit(solution)/shard_map/ppermute | solution.py:118
  8.7 78.3 %collective-permute-start.7 = (bf16[128,256]{0,1:T(8,128)(2,1)S(1)}, bf16[128,256]{0,1:T(8,128)(2,1)S(1)}, u32[]{:S(2)}, u32[]{:S(2)}) collective-permute-start(bf16[128,256]{0,1:T(8,128)(2,1)S(1)} %bitcast.108), channel_id=1, source_target_pairs={{0,4},{4,8},{8,12},{12,16},{16,20},{20,24},{24,28},{1,5},{5,9},{9,... | collective-permute-start | bytes 196616 | tf_op jit(solution)/shard_map/ppermute | solution.py:15
  12.2 75.2 %collective-permute-start.8 = (bf16[128,256]{1,0:T(8,128)(2,1)}, bf16[128,256]{1,0:T(8,128)(2,1)S(1)}, u32[]{:S(2)}, u32[]{:S(2)}) collective-permute-start(bf16[128,256]{1,0:T(8,128)(2,1)} %param.10), channel_id=1, source_target_pairs={{0,4},{4,8},{8,12},{12,16},{16,20},{20,24},{24,28},{1,5},{5,9},{9,... | collective-permute-start | bytes 196616 | tf_op jit(solution)/shard_map/ppermute | solution.py:15
  16.4 32.2 %all-to-all-start = ((bf16[4,32,256]{2,1,0:T(8,128)(2,1)}), bf16[4,32,256]{2,1,0:T(8,128)(2,1)S(1)}, u32[]{:S(2)}, u32[]{:S(2)}) async-start(bf16[4,32,256]{2,1,0:T(8,128)(2,1)} %convert_element_type.70), calls=%async_computation | async-start | bytes 131072 | tf_op jit(solution)/shard_map/all_to_all | solution.py:147
  19.8 14.8 %copy-start.2 = (s32[8]{0:T(128)S(1)}, s32[8]{0:T(128)}, u32[]{:S(2)}) copy-start(s32[8]{0:T(128)} %param.15) | copy-start | bytes 100
  19.8 32.0 %copy-start.1 = (bf16[64,256]{1,0:T(8,128)(2,1)S(1)}, bf16[64,256]{1,0:T(8,128)(2,1)}, u32[]{:S(2)}) copy-start(bf16[64,256]{1,0:T(8,128)(2,1)} %param.12) | copy-start | bytes 98308
  20.5 7.2 %collective-permute-start.1 = (bf16[64,256]{0,1:T(8,128)(2,1)S(1)}, bf16[64,256]{0,1:T(8,128)(2,1)S(1)}, u32[]{:S(2)}, u32[]{:S(2)}) collective-permute-start(bf16[64,256]{0,1:T(8,128)(2,1)S(1)} %collective-permute-done), channel_id=1, source_target_pairs={{0,4},{4,8},{8,12},{12,16},{16,20},{20,24},{24,28},{28,0},{1,5},{5... | collective-permute-start | bytes 98312 | tf_op jit(solution)/shard_map/ppermute | solution.py:118
  27.7 7.0 %collective-permute-start.2 = (bf16[64,256]{0,1:T(8,128)(2,1)S(1)}, bf16[64,256]{0,1:T(8,128)(2,1)S(1)}, u32[]{:S(2)}, u32[]{:S(2)}) collective-permute-start(bf16[64,256]{0,1:T(8,128)(2,1)S(1)} %collective-permute-done.1), channel_id=1, source_target_pairs={{0,4},{4,8},{8,12},{12,16},{16,20},{20,24},{24,28},{28,0},{1,5},{5... | collective-permute-start | bytes 98312 | tf_op jit(solution)/shard_map/ppermute | solution.py:118
  34.6 7.0 %collective-permute-start.3 = (bf16[64,256]{0,1:T(8,128)(2,1)S(1)}, bf16[64,256]{0,1:T(8,128)(2,1)S(1)}, u32[]{:S(2)}, u32[]{:S(2)}) collective-permute-start(bf16[64,256]{0,1:T(8,128)(2,1)S(1)} %collective-permute-done.2), channel_id=1, source_target_pairs={{0,4},{4,8},{8,12},{12,16},{16,20},{20,24},{24,28},{28,0},{1,5},{5... | collective-permute-start | bytes 98312 | tf_op jit(solution)/shard_map/ppermute | solution.py:118
  41.6 7.0 %collective-permute-start.4 = (bf16[64,256]{0,1:T(8,128)(2,1)S(1)}, bf16[64,256]{0,1:T(8,128)(2,1)S(1)}, u32[]{:S(2)}, u32[]{:S(2)}) collective-permute-start(bf16[64,256]{0,1:T(8,128)(2,1)S(1)} %collective-permute-done.3), channel_id=1, source_target_pairs={{0,4},{4,8},{8,12},{12,16},{16,20},{20,24},{24,28},{28,0},{1,5},{5... | collective-permute-start | bytes 98312 | tf_op jit(solution)/shard_map/ppermute | solution.py:118
  48.6 36.5 %collective-permute-start.5 = (bf16[64,256]{0,1:T(8,128)(2,1)S(1)}, bf16[64,256]{0,1:T(8,128)(2,1)S(1)}, u32[]{:S(2)}, u32[]{:S(2)}) collective-permute-start(bf16[64,256]{0,1:T(8,128)(2,1)S(1)} %collective-permute-done.4), channel_id=1, source_target_pairs={{0,4},{4,8},{8,12},{12,16},{16,20},{20,24},{24,28},{28,0},{1,5},{5... | collective-permute-start | bytes 98312 | tf_op jit(solution)/shard_map/ppermute | solution.py:118
  48.6 35.8 %all-to-all-start.1 = ((bf16[4,32,256]{2,1,0:T(8,128)(2,1)}), bf16[4,32,256]{2,1,0:T(8,128)(2,1)S(1)}, u32[]{:S(2)}, u32[]{:S(2)}) async-start(bf16[4,32,256]{2,1,0:T(8,128)(2,1)} %bitcast.29), calls=%async_computation.1 | async-start | bytes 131072 | tf_op jit(solution)/shard_map/all_to_all | solution.py:148
  85.0 7.0 %collective-permute-start.6 = (bf16[64,256]{0,1:T(8,128)(2,1)S(1)}, bf16[64,256]{0,1:T(8,128)(2,1)S(1)}, u32[]{:S(2)}, u32[]{:S(2)}) collective-permute-start(bf16[64,256]{0,1:T(8,128)(2,1)S(1)} %collective-permute-done.5), channel_id=1, source_target_pairs={{0,4},{4,8},{8,12},{12,16},{16,20},{20,24},{24,28},{28,0},{1,5},{5... | collective-permute-start | bytes 98312 | tf_op jit(solution)/shard_map/ppermute | solution.py:118
